TPU v7x, 32 devices: a whole 2x2x4 slice. The times are simulated.
32 devices in a mesh: seq: 4 (over z), ch: 8 (over y, x, core).
Axes of the slice: x: 2, y: 2, z: 4, core: 2. Of those that a mesh axis runs over, the one named last changes fastest.
Arguments:
- inputs: bfloat16 [1024, 8192], P('seq', 'ch'), may hold values from -6 to 6
- w_in: bfloat16 [3, 8192, 8192], P(None, 'seq', 'ch'), may hold values from -0.0625 to 0.0625
- short_filter: float32 [3, 3, 8192], P(None, None, 'ch'), may hold values from -3 to 3
- rates: float32 [16, 8192], P(None, 'ch'), may hold values from 9.765625e-05 to 0.05
- residues: float32 [16, 8192], P(None, 'ch'), may hold values from -3 to 3
- skip: float32 [8192], P('ch'), may hold values from -3 to 3
Outputs:
- gated: bfloat16 [1024, 8192], P('seq', 'ch')
All inputs are finite; a program needn't handle non-finite values.
Results may differ from a plain program's by a relative error of at most 0.0065.
Values may be sent and summed in bfloat16 or wider, within the bound.
No kernel may reach another device: no remote copies, remote signals or barrier semaphores. Data moves between devices by JAX's collectives and lax.ppermute only.
A program may use at most 128 MiB of HBM per device.

v0:
```python
import jax
import jax.numpy as jnp
from jax import lax
from jax.sharding import PartitionSpec as P

TAPS = 3


def passed_along(block, axis, distance):
    devices = range(lax.axis_size(axis))
    route = [(i - distance, i) for i in devices if i - distance in devices]
    return lax.ppermute(block, axis, route)


def carried_in(part, axis, combine, identity):
    place = lax.axis_index(axis)
    gathered = jax.tree.map(lambda a: lax.all_gather(a, axis), part)
    state = jax.tree.map(lambda a, e: jnp.zeros_like(a) + jnp.asarray(e, a.dtype), part, identity)

    def one(hop, state):
        return combine(
            state, jax.tree.map(lambda a: lax.dynamic_index_in_dim(a, hop, 0, False), gathered)
        )

    return lax.fori_loop(0, place, one, state)


def combine(earlier, later):
    return (earlier[0] * later[0], earlier[1] * later[0] + later[1])


def project(inputs, w_in):
    tok_rows = inputs.shape[0]
    n_seq = lax.axis_size("seq")
    n_ch = lax.axis_size("ch")
    features = lax.all_gather(inputs, "ch", axis=1, tiled=True)
    piece = features.shape[1] // (n_seq * n_ch)
    features = features.reshape(tok_rows, n_seq, n_ch, piece)
    mine = lax.dynamic_index_in_dim(features, lax.axis_index("ch"), 2, False)
    rows = lax.all_to_all(mine, "seq", 1, 0, tiled=True)
    rows = rows.reshape(n_seq * tok_rows, piece)
    block = lax.all_gather(rows, "ch", axis=1, tiled=True)
    partial = jnp.einsum("td,kdc->ktc", block, w_in, preferred_element_type=jnp.float32)
    return lax.psum_scatter(partial, "seq", scatter_dimension=1, tiled=True)


def per_device(inputs, w_in, short_filter, rates, residues, skip):
    tok_rows = inputs.shape[0]
    width = w_in.shape[2]
    modes = rates.shape[0]
    proj = project(inputs, w_in).astype(jnp.bfloat16)
    prior = passed_along(proj[:, tok_rows - (TAPS - 1) :, :], "seq", 1)
    padded = jnp.concatenate([prior, proj], axis=1).astype(jnp.float32)
    mixed = jnp.zeros((3, tok_rows, width), jnp.float32)
    for j in range(TAPS):
        mixed = (
            mixed
            + short_filter[:, j, None, :] * padded[:, TAPS - 1 - j : TAPS - 1 - j + tok_rows, :]
        )
    query, key, value = (mixed[0], mixed[1], mixed[2])
    drive = key * value
    position = jnp.arange(tok_rows, dtype=jnp.float32)
    scaled = residues * jnp.sqrt(1.0 - jnp.exp(-2.0 * rates))
    end_powers = jnp.exp(-rates[None, :, :] * (tok_rows - 1.0 - position)[:, None, None])
    end_state = jnp.sum(end_powers * drive[:, None, :], axis=0)
    block_decay = jnp.exp(-rates * tok_rows)
    identity = (jnp.ones_like(block_decay), jnp.zeros_like(end_state))
    entering = carried_in((block_decay, end_state), "seq", combine, identity)[1]
    start_powers = jnp.exp(-rates[None, :, :] * (position + 1.0)[:, None, None])
    cross = jnp.sum(start_powers * (scaled * entering)[None, :, :], axis=1)
    center = (tok_rows - 1.0) / 2.0
    offset = (position - center)[:, None, None]
    rising = jnp.exp(rates[None, :, :] * offset) * drive[:, None, :]
    offsets = jnp.arange(tok_rows, dtype=jnp.int32)
    lower = (offsets[:, None] >= offsets[None, :]).astype(jnp.float32)
    prefix = jnp.dot(
        lower, rising.reshape(tok_rows, modes * width), precision=lax.Precision.HIGHEST
    )
    prefix = prefix.reshape(tok_rows, modes, width)
    falling = jnp.exp(-rates[None, :, :] * offset) * scaled[None, :, :]
    local = jnp.sum(falling * prefix, axis=1)
    return (query * (local + cross + skip[None, :] * drive)).astype(jnp.bfloat16)


def solution(mesh):
    in_specs = (
        P("seq", "ch"),
        P(None, "seq", "ch"),
        P(None, None, "ch"),
        P(None, "ch"),
        P(None, "ch"),
        P("ch"),
    )
    out_specs = P("seq", "ch")
    return jax.shard_map(
        per_device, mesh=mesh, in_specs=in_specs, out_specs=out_specs, check_vma=False
    )
```

profile of v0, /device:TPU:26, one launch (start us, length us, event | category | flops | bytes accessed | tf_op | source)
XLA Modules:
  0.0 415.0 jit_solution(5616361309072354084)
XLA Ops:
  7.3 39.5 %all-gather.5.cloned.1.call-done = bf16[256,8192]{1,0:T(8,128)(2,1)} async-done(((bf16[256,1024]{1,0:T(8,128)(2,1)}), bf16[256,8192]{1,0:T(8,128)(2,1)}) %all-gather.5.cloned.1.call-update) | async-done | bytes 4194320 | tf_op jit(solution)/shard_map/all_gather | solution.py:36
  46.8 3.6 copy.15
  50.4 1.1 constant_dynamic-slice_fusion
  51.7 17.5 %all_to_all.15 = bf16[256,4,256]{2,0,1:T(8,128)(2,1)} all-to-all(bf16[256,4,256]{2,0,1:T(8,128)(2,1)S(1)} %bitcast.60), channel_id=1, replica_groups=mesh['seq'=4,'ch'=8] {'seq'}, dimensions={1} | all-to-all | bytes 1048576 | tf_op jit(solution)/shard_map/all_to_all | solution.py:40
  69.3 37.4 %all-gather.7.cloned.1.call-done = bf16[1024,2048]{1,0:T(8,128)(2,1)} async-done(((bf16[1024,256]{1,0:T(8,128)(2,1)}), bf16[1024,2048]{1,0:T(8,128)(2,1)}) %all-gather.7.cloned.1.call-update) | async-done | bytes 4194320 | tf_op jit(solution)/shard_map/all_gather | solution.py:42
  106.7 18.9 %convolution_bitcast_fusion = f32[3,1024,1024]{2,1,0:T(8,128)} fusion(bf16[3,2048,1024]{2,1,0:T(8,128)(2,1)} %param.9, bf16[1024,2048]{1,0:T(8,128)(2,1)} %all-gather.7.cloned.1.call-done), kind=kOutput, calls=%fused_computation.6 | convolution fusion | flops 12884901888 | bytes 29360128 | tf_op jit(solution)/shard_map/td,kdc->ktc/dot_general | solution.py:43
  127.1 210.6 %reduce-scatter.2.cloned.1.call-done = f32[3,256,1024]{2,1,0:T(8,128)} async-done(((f32[3,1024,1024]{2,1,0:T(8,128)}), f32[3,256,1024]{2,1,0:T(8,128)}) %reduce-scatter.2.cloned.1.call-update) | async-done | bytes 3145744 | tf_op jit(solution)/shard_map/reduce_scatter | solution.py:44
  337.7 2.1 convert_element_type.10
  339.9 1.3 collective-permute-start
  341.2 15.8 %all-gather = f32[64,1024]{1,0:T(8,128)S(1)} all-gather(f32[16,1024]{1,0:T(8,128)S(1)} %get-tuple-element.63), channel_id=2, replica_groups=mesh['seq'=4,'ch'=8] {'seq'}, dimensions={0}, use_global_device_ids=true | all-gather | bytes 327680 | tf_op jit(solution)/shard_map/all_gather | solution.py:17
  358.1 0.9 fusion.1
  359.0 1.2 fusion.3
  360.2 2.5 copy.14
  362.7 4.1 multiply_reduce_fusion.1
  366.8 14.6 %all-gather.1 = f32[64,1024]{1,0:T(8,128)} all-gather(f32[16,1024]{1,0:T(8,128)S(1)} %multiply_reduce_fusion.1), channel_id=3, replica_groups=mesh['seq'=4,'ch'=8] {'seq'}, dimensions={0}, use_global_device_ids=true | all-gather | bytes 327680 | tf_op jit(solution)/shard_map/all_gather | solution.py:17
  381.4 2.9 while.12
  381.4 0.9 bitcast_add_fusion.2
  382.3 0.9 bitcast_add_fusion.2
  383.2 0.9 bitcast_add_fusion.2
  384.3 0.9 fusion.8
  385.2 3.9 bitcast_multiply_fusion.1
  389.2 13.9 %multiply_reduce_fusion.2 = f32[256,1024]{1,0:T(8,128)} fusion(f32[16,1024,256]{2,1,0:T(8,128)S(1)} %bitcast.57, f32[16,1024]{1,0:T(8,128)S(1)} %get-tuple-element.61, f32[256]{0:T(256)S(1)} %iota_add_fusion.1, f32[16,1024]{1,0:T(8,128)S(1)} %copy-done.1), kind=kOutput, calls=%fused_computation.5 | convolution fusion | flops 12901482496 | bytes 17957888 | tf_op jit(solution)/shard_map/dot_general | solution.py:76
  403.1 2.8 multiply_reduce_fusion
  405.9 2.6 fusion.5
  (27 shorter events, 3.6 us)
Async XLA Ops:
  6.5 40.3 %all-gather.5.cloned.1.call-start = ((), (), s32[]{:S(2)}) async-start(), calls=%async_computation.2 | async-start | bytes 4718592 | tf_op jit(solution)/shard_map/all_gather | solution.py:36
  7.3 99.5 %all-gather.7.cloned.1.call-start = ((), (), s32[]{:S(2)}) async-start(), calls=%async_computation.3 | async-start | bytes 4718592 | tf_op jit(solution)/shard_map/all_gather | solution.py:42
  69.2 268.5 %reduce-scatter.2.cloned.1.call-start = ((), (), s32[]{:S(2)}) async-start(), calls=%async_computation.4 | async-start | bytes 15728640 | tf_op jit(solution)/shard_map/reduce_scatter | solution.py:44
  125.6 0.8 copy-start.2
  125.6 0.9 copy-start
  339.9 17.7 %collective-permute-start = (bf16[3,2,1024]{2,1,0:T(2,128)(2,1)S(1)}, bf16[3,2,1024]{2,1,0:T(2,128)(2,1)S(1)}, u32[]{:S(2)}, u32[]{:S(2)}) collective-permute-start(bf16[3,2,1024]{2,1,0:T(2,128)(2,1)S(1)} %slice.40), channel_id=1, source_target_pairs={{0,8},{8,16},{16,24},{1,9},{9,17},{17,25},{2,10},{10,18},{18,26},{... | collective-permute-start | bytes 36872 | tf_op jit(solution)/shard_map/ppermute | solution.py:12
  384.3 4.8 %copy-start.1 = (f32[16,1024]{1,0:T(8,128)S(1)}, f32[16,1024]{1,0:T(8,128)}, u32[]{:S(2)}) copy-start(f32[16,1024]{1,0:T(8,128)} %get-tuple-element.62) | copy-start | bytes 196612
  389.1 16.7 %copy-start.3 = (f32[1024]{0:T(1024)S(1)}, f32[1024]{0:T(1024)}, u32[]{:S(2)}) copy-start(f32[1024]{0:T(1024)} %param.13) | copy-start | bytes 12292
Sparse Core Ops, SparseCore 0:
  9.2 37.5 all-gather.4
  69.3 37.3 all-gather.6
  125.8 211.8 reduce-scatter.1
where the time goes:
time: 416 us; the launch traced here: 415 us
  waiting for transfers between devices  288 us (69%)
  blocking collectives  47.9 us (12%)
  matrix products  32.8 us (8%)
  other arithmetic  22.3 us (5%)
  between operations  13.3 us (3%)
  local copies, waits for them, and re-layouts  8.82 us (2%)
    reduce_scatter x1, waiting for transfers between devices, project(): return lax.psum_scatter(partial, 'seq', scatter_dimension=1, tiled=True)  211 us
    all_gather x1, waiting for transfers between devices, project(): features = lax.all_gather(inputs, 'ch', axis=1, tiled=True)  39.5 us
    all_gather x1, waiting for transfers between devices, project(): block = lax.all_gather(rows, 'ch', axis=1, tiled=True)  37.4 us
    all_gather x2, blocking collectives, carried_in(): gathered = jax.tree.map(lambda a: lax.all_gather(a, axis), part)  30.4 us
    dot_general x1, matrix products, project(): jnp.einsum('td,kdc->ktc', block, w_in, preferred_element_type=jnp.float32)  18.9 us
    all_to_all x1, blocking collectives, project(): rows = lax.all_to_all(mine, 'seq', 1, 0, tiled=True)  17.5 us
    dot_general x1, matrix products, per_device(): jnp.dot(lower, rising.reshape(tok_rows, modes * width), precision=lax.Pre...  13.9 us
  transfers between devices with their start and end apart: 4, of which 3 were waited for; matrix products, arithmetic and copies ran while one was open for 0% of the time, Pallas kernels for 0%

commit v1 on v0

--- a/solution.py
+++ b/solution.py
@@ -39,7 +39,28 @@
     mine = lax.dynamic_index_in_dim(features, lax.axis_index("ch"), 2, False)
     rows = lax.all_to_all(mine, "seq", 1, 0, tiled=True)
     rows = rows.reshape(n_seq * tok_rows, piece)
-    block = lax.all_gather(rows, "ch", axis=1, tiled=True)
+    last = lax.axis_size("ch")
+    latest, block_next, b_next = (last, lax.axis_index("ch"), rows.shape[1])
+    buffer = []
+    for src_i in range(latest):
+        buffer.append((src_i, (src_i + 1) % latest))
+    entries = []
+    for src_i in range(latest):
+        entries.append((src_i, (src_i - 1) % latest))
+    block = jnp.zeros((*rows.shape[:1], latest * b_next, *rows.shape[2:]), rows.dtype)
+    block = lax.dynamic_update_slice_in_dim(block, rows, block_next * b_next, axis=1)
+    part_now = before = rows
+    back = latest // 2
+    for d in range(1, back + 1):
+        part_now = lax.ppermute(part_now, perm=buffer, axis_name="ch")
+        block = lax.dynamic_update_slice_in_dim(
+            block, part_now, (block_next - d) % latest * b_next, axis=1
+        )
+        if d < latest - back:
+            before = lax.ppermute(before, axis_name="ch", perm=entries)
+            block = lax.dynamic_update_slice_in_dim(
+                block, before, (block_next + d) % latest * b_next, axis=1
+            )
     partial = jnp.einsum("td,kdc->ktc", block, w_in, preferred_element_type=jnp.float32)
     return lax.psum_scatter(partial, "seq", scatter_dimension=1, tiled=True)
 

time: 416 us -> 424 us (1.019)
  starting transfers between devices: 1.37 us -> 20 us
  waiting for transfers between devices: 288 us -> 282 us
    all_gather x1 -> x0, waiting for transfers between devices: 37.4 us -> none  [project(): block = lax.all_gather(rows, 'ch', axis=1, tiled=True)]
    ppermute x0 -> x7, waiting for transfers between devices: none -> 26.2 us  [the longest x4 25.7 us: project(): part_now = lax.ppermute(part_now, perm=buffer, axis_name='ch')]
    ppermute x0 -> x7, starting transfers between devices: none -> 18.7 us  [the longest x4 13.4 us: project(): part_now = lax.ppermute(part_now, perm=buffer, axis_name='ch')]
    reduce_scatter x1, waiting for transfers between devices: 211 us -> 218 us  [project(): return lax.psum_scatter(partial, 'seq', scatter_dimension=1, tiled=True)]
  transfers between devices with their start and end apart: 4 -> 10, of which waited for: 3 -> 7; matrix products, arithmetic and copies ran while one was open for 0% -> 1% of each run, Pallas kernels for 0% -> 0%
where the time goes in v1:
time: 424 us; the launch traced here: 423 us
  waiting for transfers between devices  282 us (67%)
  blocking collectives  47.8 us (11%)
  matrix products  29.5 us (7%)
  other arithmetic  21 us (5%)
  starting transfers between devices  20 us (5%)
  between operations  13.7 us (3%)
  local copies, waits for them, and re-layouts  8.38 us (2%)
    reduce_scatter x1, waiting for transfers between devices, project(): return lax.psum_scatter(partial, 'seq', scatter_dimension=1, tiled=True)  218 us
    all_gather x1, waiting for transfers between devices, project(): features = lax.all_gather(inputs, 'ch', axis=1, tiled=True)  38.1 us
    all_gather x2, blocking collectives, carried_in(): gathered = jax.tree.map(lambda a: lax.all_gather(a, axis), part)  30.4 us
    ppermute x4, waiting for transfers between devices, project(): part_now = lax.ppermute(part_now, perm=buffer, axis_name='ch')  25.7 us
    all_to_all x1, blocking collectives, project(): rows = lax.all_to_all(mine, 'seq', 1, 0, tiled=True)  17.4 us
    dot_general x1, matrix products, project(): jnp.einsum('td,kdc->ktc', block, w_in, preferred_element_type=jnp.float32)  15.5 us
    dot_general x1, matrix products, per_device(): jnp.dot(lower, rising.reshape(tok_rows, modes * width), precision=lax.Pre...  14 us
    ppermute x4, starting transfers between devices, project(): part_now = lax.ppermute(part_now, perm=buffer, axis_name='ch')  13.4 us
  transfers between devices with their start and end apart: 10, of which 7 were waited for; matrix products, arithmetic and copies ran while one was open for 1% of the time, Pallas kernels for 0%

profile of v1, /device:TPU:26, one launch (start us, length us, event | category | flops | bytes accessed | tf_op | source)
XLA Modules:
  0.0 422.7 jit_solution(1415495555207602423)
XLA Ops:
  6.5 2.0 copy.8
  8.7 38.1 %all-gather.4.cloned.1.call-done = bf16[256,8192]{0,1:T(8,128)(2,1)} async-done(((bf16[256,1024]{0,1:T(8,128)(2,1)}), bf16[256,8192]{0,1:T(8,128)(2,1)}) %all-gather.4.cloned.1.call-update) | async-done | bytes 4194320 | tf_op jit(solution)/shard_map/all_gather | solution.py:36
  48.1 17.4 %all_to_all.15 = bf16[256,4,256]{2,0,1:T(8,128)(2,1)S(1)} all-to-all(bf16[256,4,256]{2,0,1:T(8,128)(2,1)S(1)} %bitcast.57), channel_id=1, replica_groups=mesh['seq'=4,'ch'=8] {'seq'}, dimensions={1} | all-to-all | bytes 1048576 | tf_op jit(solution)/shard_map/all_to_all | solution.py:40
  65.5 1.7 collective-permute-start.1
  67.3 10.7 %collective-permute-done = bf16[1024,256]{1,0:T(8,128)(2,1)S(1)} collective-permute-done((bf16[1024,256]{1,0:T(8,128)(2,1)S(1)}, bf16[1024,256]{1,0:T(8,128)(2,1)S(1)}, u32[]{:S(2)}, u32[]{:S(2)}) %collective-permute-start) | collective-permute-done | bytes 524320 | tf_op jit(solution)/shard_map/ppermute | solution.py:55
  78.5 1.9 collective-permute-start.3
  80.5 8.2 %collective-permute-done.2 = bf16[1024,256]{1,0:T(8,128)(2,1)S(1)} collective-permute-done((bf16[1024,256]{1,0:T(8,128)(2,1)S(1)}, bf16[1024,256]{1,0:T(8,128)(2,1)S(1)}, u32[]{:S(2)}, u32[]{:S(2)}) %collective-permute-start.2) | collective-permute-done | bytes 524320 | tf_op jit(solution)/shard_map/ppermute | solution.py:55
  88.6 4.0 collective-permute-start.4
  93.2 1.6 collective-permute-start.5
  94.9 2.9 collective-permute-done.4
  97.8 9.5 %collective-permute-start.6 = (bf16[1024,256]{1,0:T(8,128)(2,1)S(1)}, bf16[1024,256]{1,0:T(8,128)(2,1)S(1)}, u32[]{:S(2)}, u32[]{:S(2)}) collective-permute-start(bf16[1024,256]{1,0:T(8,128)(2,1)S(1)} %collective-permute-done.4), channel_id=1, source_target_pairs={{0,1},{1,2},{2,3},{3,4},{4,5},{5,6},{6,7},{7,0},{8,9},{9,10},{10,1... | collective-permute-start | bytes 1572872 | tf_op jit(solution)/shard_map/ppermute | solution.py:55
  107.7 3.8 collective-permute-done.6
  111.6 15.5 %convolution_bitcast_fusion = f32[3,1024,1024]{2,1,0:T(8,128)} fusion(bf16[3,2048,1024]{2,1,0:T(8,128)(2,1)S(1)} %copy-done.6, bf16[1024,2048]{1,0:T(8,128)(2,1)S(1)} %constant_dynamic-update-slice_fusion), kind=kOutput, calls=%fused_computation.6 | convolution fusion | flops 12884901888 | bytes 29360128 | tf_op jit(solution)/shard_map/td,kdc->ktc/dot_general | solution.py:64
  128.6 217.7 %reduce-scatter.2.cloned.1.call-done = f32[3,256,1024]{2,1,0:T(8,128)} async-done(((f32[3,1024,1024]{2,1,0:T(8,128)}), f32[3,256,1024]{2,1,0:T(8,128)}) %reduce-scatter.2.cloned.1.call-update) | async-done | bytes 3145744 | tf_op jit(solution)/shard_map/reduce_scatter | solution.py:65
  346.2 2.1 convert_element_type.10
  349.7 15.8 %all-gather = f32[64,1024]{1,0:T(8,128)S(1)} all-gather(f32[16,1024]{1,0:T(8,128)S(1)} %get-tuple-element.63), channel_id=2, replica_groups=mesh['seq'=4,'ch'=8] {'seq'}, dimensions={0}, use_global_device_ids=true | all-gather | bytes 327680 | tf_op jit(solution)/shard_map/all_gather | solution.py:17
  368.7 2.5 copy.15
  371.2 4.1 multiply_reduce_fusion.1
  375.3 14.6 %all-gather.1 = f32[64,1024]{1,0:T(8,128)} all-gather(f32[16,1024]{1,0:T(8,128)S(1)} %multiply_reduce_fusion.1), channel_id=3, replica_groups=mesh['seq'=4,'ch'=8] {'seq'}, dimensions={0}, use_global_device_ids=true | all-gather | bytes 327680 | tf_op jit(solution)/shard_map/all_gather | solution.py:17
  390.0 2.9 while.12
  393.7 3.9 bitcast_multiply_fusion.1
  397.7 14.0 %multiply_reduce_fusion.2 = f32[256,1024]{1,0:T(8,128)} fusion(f32[16,1024,256]{2,1,0:T(8,128)S(1)} %bitcast.53, f32[16,1024]{1,0:T(8,128)S(1)} %get-tuple-element.61, f32[256]{0:T(256)S(1)} %iota_add_fusion.1, f32[16,1024]{1,0:T(8,128)S(1)} %copy-done.3), kind=kOutput, calls=%fused_computation.5 | convolution fusion | flops 12901482496 | bytes 17957888 | tf_op jit(solution)/shard_map/dot_general | solution.py:97
  411.7 2.8 multiply_reduce_fusion
  414.5 1.4 fusion.5
  (53 shorter events, 12.4 us)
Async XLA Ops:
  6.5 40.3 %all-gather.4.cloned.1.call-start = ((), (), s32[]{:S(2)}) async-start(), calls=%async_computation.2 | async-start | bytes 4718592 | tf_op jit(solution)/shard_map/all_gather | solution.py:36
  8.6 337.6 %reduce-scatter.2.cloned.1.call-start = ((), (), s32[]{:S(2)}) async-start(), calls=%async_computation.3 | async-start | bytes 15728640 | tf_op jit(solution)/shard_map/reduce_scatter | solution.py:65
  65.5 12.5 %collective-permute-start = (bf16[1024,256]{1,0:T(8,128)(2,1)S(1)}, bf16[1024,256]{1,0:T(8,128)(2,1)S(1)}, u32[]{:S(2)}, u32[]{:S(2)}) collective-permute-start(bf16[1024,256]{1,0:T(8,128)(2,1)S(1)} %bitcast.54), channel_id=1, source_target_pairs={{0,1},{1,2},{2,3},{3,4},{4,5},{5,6},{6,7},{7,0},{8,9},{9,10},{10,1... | collective-permute-start | bytes 1572872 | tf_op jit(solution)/shard_map/ppermute | solution.py:55
  65.5 13.0 %collective-permute-start.1 = (bf16[1024,256]{1,0:T(8,128)(2,1)S(1)}, bf16[1024,256]{1,0:T(8,128)(2,1)S(1)}, u32[]{:S(2)}, u32[]{:S(2)}) collective-permute-start(bf16[1024,256]{1,0:T(8,128)(2,1)S(1)} %bitcast.55), channel_id=1, source_target_pairs={{0,7},{1,0},{2,1},{3,2},{4,3},{5,4},{6,5},{7,6},{8,15},{9,8},{10,9... | collective-permute-start | bytes 1572872 | tf_op jit(solution)/shard_map/ppermute | solution.py:60
  78.0 10.7 %collective-permute-start.2 = (bf16[1024,256]{1,0:T(8,128)(2,1)S(1)}, bf16[1024,256]{1,0:T(8,128)(2,1)S(1)}, u32[]{:S(2)}, u32[]{:S(2)}) collective-permute-start(bf16[1024,256]{1,0:T(8,128)(2,1)S(1)} %collective-permute-done), channel_id=1, source_target_pairs={{0,1},{1,2},{2,3},{3,4},{4,5},{5,6},{6,7},{7,0},{8,9},{9,10},{10,1... | collective-permute-start | bytes 1572872 | tf_op jit(solution)/shard_map/ppermute | solution.py:55
  78.5 14.7 %collective-permute-start.3 = (bf16[1024,256]{1,0:T(8,128)(2,1)S(1)}, bf16[1024,256]{1,0:T(8,128)(2,1)S(1)}, u32[]{:S(2)}, u32[]{:S(2)}) collective-permute-start(bf16[1024,256]{1,0:T(8,128)(2,1)S(1)} %collective-permute-done.1), channel_id=1, source_target_pairs={{0,7},{1,0},{2,1},{3,2},{4,3},{5,4},{6,5},{7,6},{8,15},{9,8},{10,9... | collective-permute-start | bytes 1572872 | tf_op jit(solution)/shard_map/ppermute | solution.py:60
  88.6 9.2 %collective-permute-start.4 = (bf16[1024,256]{1,0:T(8,128)(2,1)S(1)}, bf16[1024,256]{1,0:T(8,128)(2,1)S(1)}, u32[]{:S(2)}, u32[]{:S(2)}) collective-permute-start(bf16[1024,256]{1,0:T(8,128)(2,1)S(1)} %collective-permute-done.2), channel_id=1, source_target_pairs={{0,1},{1,2},{2,3},{3,4},{4,5},{5,6},{6,7},{7,0},{8,9},{9,10},{10,1... | collective-permute-start | bytes 1572872 | tf_op jit(solution)/shard_map/ppermute | solution.py:55
  92.6 18.9 %copy-start.6 = (bf16[3,2048,1024]{2,1,0:T(8,128)(2,1)S(1)}, bf16[3,2048,1024]{2,1,0:T(8,128)(2,1)}, u32[]{:S(2)}) copy-start(bf16[3,2048,1024]{2,1,0:T(8,128)(2,1)} %param.9) | copy-start | bytes 37748740
  93.2 14.3 %collective-permute-start.5 = (bf16[1024,256]{1,0:T(8,128)(2,1)S(1)}, bf16[1024,256]{1,0:T(8,128)(2,1)S(1)}, u32[]{:S(2)}, u32[]{:S(2)}) collective-permute-start(bf16[1024,256]{1,0:T(8,128)(2,1)S(1)} %collective-permute-done.3), channel_id=1, source_target_pairs={{0,7},{1,0},{2,1},{3,2},{4,3},{5,4},{6,5},{7,6},{8,15},{9,8},{10,9... | collective-permute-start | bytes 1572872 | tf_op jit(solution)/shard_map/ppermute | solution.py:60
  97.8 13.7 %collective-permute-start.6 = (bf16[1024,256]{1,0:T(8,128)(2,1)S(1)}, bf16[1024,256]{1,0:T(8,128)(2,1)S(1)}, u32[]{:S(2)}, u32[]{:S(2)}) collective-permute-start(bf16[1024,256]{1,0:T(8,128)(2,1)S(1)} %collective-permute-done.4), channel_id=1, source_target_pairs={{0,1},{1,2},{2,3},{3,4},{4,5},{5,6},{6,7},{7,0},{8,9},{9,10},{10,1... | collective-permute-start | bytes 1572872 | tf_op jit(solution)/shard_map/ppermute | solution.py:55
  127.1 0.8 copy-start.4
  127.1 0.9 copy-start.1
  348.4 17.7 %collective-permute-start.7 = (bf16[3,2,1024]{2,1,0:T(2,128)(2,1)S(1)}, bf16[3,2,1024]{2,1,0:T(2,128)(2,1)S(1)}, u32[]{:S(2)}, u32[]{:S(2)}) collective-permute-start(bf16[3,2,1024]{2,1,0:T(2,128)(2,1)S(1)} %slice.40), channel_id=1, source_target_pairs={{0,8},{8,16},{16,24},{1,9},{9,17},{17,25},{2,10},{10,18},{18,26},{... | collective-permute-start | bytes 36872 | tf_op jit(solution)/shard_map/ppermute | solution.py:12
  367.5 3.7 copy-start.2
  393.7 3.9 copy-start.3
  411.7 2.8 copy-start
  411.7 2.8 copy-start.5
Sparse Core Ops, SparseCore 0:
  9.2 37.5 all-gather.3
  127.2 218.9 reduce-scatter.1
